TPU v7x, 256 devices: a whole 4x4x8 slice. The times are simulated.
256 devices in a mesh: sub: 16 (over z, core), fr: 16 (over y, x).
Axes of the slice: x: 4, y: 4, z: 8, core: 2. Of those that a mesh axis runs over, the one named last changes fastest.
Arguments:
- front_leaf: bfloat16 [32768, 2048], P(('sub', 'fr')), as said below
- shares_one: float32 [32768, 384], P(('sub', 'fr')), as said below
- shares_two: float32 [32768, 384], P(('sub', 'fr')), as said below
- map_leaf: int32 [16, 13], P('sub'), may hold values from 0 to 15, as said below
- map_mid: int32 [8, 13], replicated, may hold values from 0 to 15, as said below
Outputs:
- leaf_panel: float32 [32768, 384], P(('sub', 'fr'))
- middle_panel: float32 [32768, 384], P(('sub', 'fr'))
- top_panel: float32 [32768, 384], P(('sub', 'fr'))
- contribution: float32 [32768, 1664], P(('sub', 'fr'))
Inputs may be any that keep to these rules, and one draw needn't show every extreme that they name: `front_leaf`: each block of 2048 rows is a symmetric positive definite front. `shares_one`: in each block of 2048 rows the first 384 rows are symmetric; with the extended contributions every middle front is positive definite. `shares_two`: in each block of 2048 rows the first 384 rows are symmetric; with the extended contributions every top front is positive definite. `map_leaf`: each row lists 13 different blocks; rows 2q and 2q+1 together name every block of their parent. `map_mid`: each row lists 13 different blocks; rows 2r and 2r+1 together name every block of their parent.
All inputs are finite; a program needn't handle non-finite values.
Results may differ from a plain program's by a relative error of at most 0.0003.
Values sent between devices are 32-bit elements; how exact they have to be, the bound alone decides.
No kernel may reach another device: no remote copies, remote signals or barrier semaphores. Data moves between devices by JAX's collectives and lax.ppermute only.
A program may use at most 128 MiB of HBM per device.

v0:
```python
import jax
import jax.numpy as jnp
from jax import lax
from jax.sharding import PartitionSpec as P

BLK = 128
P_SIZE = 384
NFB = 16
NPB = 3
HIGH = lax.Precision.HIGHEST


def partner(array, axis, stride):
    return lax.ppermute(array, axis, [(i, i ^ 1 << stride) for i in range(lax.axis_size(axis))])


def eliminate(front, row_start):
    row_count, front_order = front.shape
    panels = []
    for block_index in range(NPB):
        block_low = block_index * BLK
        gathered = lax.all_gather(front[:, block_low : block_low + BLK], "fr", axis=0, tiled=True)
        row_ids = jnp.arange(front_order)
        lower_block = jnp.linalg.cholesky(gathered[block_low : block_low + BLK])
        solved = lax.linalg.triangular_solve(
            lower_block, gathered, left_side=False, lower=True, transpose_a=True
        )
        below = jnp.where((row_ids >= block_low + BLK)[:, None], solved, 0.0)
        placed = below.at[block_low : block_low + BLK].set(lower_block)
        own_below = lax.dynamic_slice_in_dim(below, row_start, row_count, 0)
        own_panel = lax.dynamic_slice_in_dim(placed, row_start, row_count, 0)
        front = front - jnp.dot(
            own_below, below.T, precision=HIGH, preferred_element_type=jnp.float32
        )
        panels.append(own_panel)
    return (jnp.concatenate(panels, axis=1), front)


def make_table(block_map):
    padded = jnp.concatenate([jnp.full((NPB,), -1, jnp.int32), block_map])
    return (padded[:, None] == jnp.arange(NFB, dtype=jnp.int32)[None, :]).astype(jnp.float32)


def extend(front, block_map, row_start):
    row_count, front_order = front.shape
    block_share = row_count // BLK
    block_table = make_table(block_map)
    padded = jnp.concatenate([jnp.full((NPB,), -1, jnp.int32), block_map])
    parents = row_start // BLK + jnp.arange(block_share)
    matches = padded[None, :] == parents[:, None]
    present = jnp.any(matches, axis=1)
    source_block = jnp.sum(jnp.where(matches, jnp.arange(NFB)[None, :], 0), axis=1)
    source_rows = (source_block[:, None] * BLK + jnp.arange(BLK)[None, :]).reshape(row_count)
    is_live = jnp.repeat(present, BLK)
    shard_rows = lax.all_gather(front, "fr", axis=0, tiled=True)
    inside = is_live & (source_rows >= 0) & (source_rows < shard_rows.shape[0])
    picked_rows = jnp.take(shard_rows, jnp.clip(source_rows, 0, shard_rows.shape[0] - 1), axis=0)
    picked_rows = jnp.where(inside[:, None], picked_rows, 0.0)
    mapped = jnp.einsum(
        "rqc,qe->rec", picked_rows.reshape(row_count, NFB, BLK), block_table, precision=HIGH
    )
    return mapped.reshape(row_count, front_order)


def combine(front, shares, block_map, row_start, level_bit):
    front_order = front.shape[1]
    piece_part = extend(front, block_map, row_start) + jnp.pad(
        shares, ((0, 0), (0, front_order - P_SIZE))
    )
    return piece_part + partner(piece_part, "sub", level_bit)


def local(front_leaf, shares_one, shares_two, map_leaf, map_mid):
    row_count = front_leaf.shape[0]
    row_start = lax.axis_index("fr") * row_count
    sub_index = lax.axis_index("sub")
    leaf_panel, child_front = eliminate(front_leaf.astype(jnp.float32), row_start)
    shares_sum = shares_two + partner(shares_two, "sub", 0)
    middle_front = combine(child_front, shares_one, map_leaf[0], row_start, 0)
    middle_panel, middle_front = eliminate(middle_front, row_start)
    pair_map = lax.dynamic_index_in_dim(map_mid, sub_index // 2, 0, keepdims=False)
    top_front = combine(middle_front, shares_sum, pair_map, row_start, 1)
    top_panel, top_front = eliminate(top_front, row_start)
    row_ids = row_start + jnp.arange(row_count)
    contribution = jnp.where((row_ids >= P_SIZE)[:, None], top_front[:, P_SIZE:], 0.0)
    return (leaf_panel, middle_panel, top_panel, contribution)


def solution(mesh):
    in_specs = (
        P(("sub", "fr"), None),
        P(("sub", "fr"), None),
        P(("sub", "fr"), None),
        P("sub", None),
        P(),
    )
    out_specs = (
        P(("sub", "fr"), None),
        P(("sub", "fr"), None),
        P(("sub", "fr"), None),
        P(("sub", "fr"), None),
    )
    return jax.shard_map(local, mesh=mesh, in_specs=in_specs, out_specs=out_specs, check_vma=False)
```

profile of v0, /device:TPU:2, one launch (start us, length us, event | category | flops | bytes accessed | tf_op | source)
XLA Modules:
  0.0 1077.1 jit_solution(2914424873114445792)
XLA Ops:
  9.3 52.5 %all-gather.12.cloned.1.call-done = f32[2048,128]{0,1:T(8,128)} async-done(((f32[128,128]{0,1:T(8,128)}), f32[2048,128]{0,1:T(8,128)}) %all-gather.12.cloned.1.call-update) | async-done | bytes 1048592 | tf_op jit(solution)/shard_map/all_gather | solution.py:22
  63.6 11.7 %cholesky.149 = f32[128,128]{1,0:T(8,128)S(1)} custom-call(f32[128,128]{1,0:T(8,128)S(1)} %fusion.29), custom_call_target="Cholesky" | custom-call | tf_op jit(solution)/shard_map/jit(cholesky)/cholesky | solution.py:24
  76.6 9.8 custom-call.13
  86.5 2.3 fusion.8
  88.7 1.8 convolution_subtract_fusion.7
  91.5 47.4 %all-gather.14.cloned.1.call-done = f32[2048,128]{0,1:T(8,128)} async-done(((f32[128,128]{0,1:T(8,128)}), f32[2048,128]{0,1:T(8,128)}) %all-gather.14.cloned.1.call-update) | async-done | bytes 1048592 | tf_op jit(solution)/shard_map/all_gather | solution.py:22
  140.7 11.7 %cholesky.160 = f32[128,128]{1,0:T(8,128)S(1)} custom-call(f32[128,128]{1,0:T(8,128)S(1)} %fusion.27), custom_call_target="Cholesky" | custom-call | tf_op jit(solution)/shard_map/jit(cholesky)/cholesky | solution.py:24
  153.8 9.8 custom-call.14
  163.6 2.3 fusion.7
  165.8 1.8 convolution_subtract_fusion.6
  169.8 47.2 %all-gather.16.cloned.1.call-done = f32[2048,128]{0,1:T(8,128)} async-done(((f32[128,128]{0,1:T(8,128)}), f32[2048,128]{0,1:T(8,128)}) %all-gather.16.cloned.1.call-update) | async-done | bytes 1048592 | tf_op jit(solution)/shard_map/all_gather | solution.py:22
  218.8 11.7 %cholesky.171 = f32[128,128]{1,0:T(8,128)S(1)} custom-call(f32[128,128]{1,0:T(8,128)S(1)} %fusion.25), custom_call_target="Cholesky" | custom-call | tf_op jit(solution)/shard_map/jit(cholesky)/cholesky | solution.py:24
  231.9 9.8 custom-call.15
  241.7 2.3 fusion.6
  244.9 4.0 convolution_subtract_fusion.5
  252.2 1.4 compare_reduce_fusion.10
  255.3 118.1 %all-gather.18.cloned.1.call-done = f32[2048,2048]{0,1:T(8,128)} async-done(((f32[128,2048]{0,1:T(8,128)}), f32[2048,2048]{0,1:T(8,128)}) %all-gather.18.cloned.1.call-update) | async-done | bytes 16777232 | tf_op jit(solution)/shard_map/all_gather | solution.py:55
  373.4 17.6 %copy.19 = f32[2048,2048]{1,0:T(8,128)} copy(f32[2048,2048]{0,1:T(8,128)} %all-gather.18.cloned.1.call-done) | data formatting | bytes 33554432 | tf_op jit(solution)/shard_map/all_gather | solution.py:55
  391.0 7.3 gather_fusion
  400.7 1.4 copy.20
  402.1 1.3 bitcast_add_fusion.1
  403.6 2.6 collective-permute-done
  407.0 47.7 %all-gather.20.cloned.1.call-done = f32[2048,128]{0,1:T(8,128)} async-done(((f32[128,128]{0,1:T(8,128)}), f32[2048,128]{0,1:T(8,128)}) %all-gather.20.cloned.1.call-update) | async-done | bytes 1048592 | tf_op jit(solution)/shard_map/all_gather | solution.py:22
  456.5 11.7 %cholesky.182 = f32[128,128]{1,0:T(8,128)S(1)} custom-call(f32[128,128]{1,0:T(8,128)S(1)} %fusion.23), custom_call_target="Cholesky" | custom-call | tf_op jit(solution)/shard_map/jit(cholesky)/cholesky | solution.py:24
  470.2 9.8 custom-call.16
  480.0 2.3 fusion.5
  482.3 1.8 convolution_subtract_fusion.4
  486.0 47.4 %all-gather.22.cloned.1.call-done = f32[2048,128]{0,1:T(8,128)} async-done(((f32[128,128]{0,1:T(8,128)}), f32[2048,128]{0,1:T(8,128)}) %all-gather.22.cloned.1.call-update) | async-done | bytes 1048592 | tf_op jit(solution)/shard_map/all_gather | solution.py:22
  535.2 11.7 %cholesky.193 = f32[128,128]{1,0:T(8,128)S(1)} custom-call(f32[128,128]{1,0:T(8,128)S(1)} %fusion.21), custom_call_target="Cholesky" | custom-call | tf_op jit(solution)/shard_map/jit(cholesky)/cholesky | solution.py:24
  548.9 9.8 custom-call.17
  558.7 2.3 fusion.4
  562.0 3.0 convolution_subtract_fusion.3
  566.1 47.2 %all-gather.24.cloned.1.call-done = f32[2048,128]{0,1:T(8,128)} async-done(((f32[128,128]{0,1:T(8,128)}), f32[2048,128]{0,1:T(8,128)}) %all-gather.24.cloned.1.call-update) | async-done | bytes 1048592 | tf_op jit(solution)/shard_map/all_gather | solution.py:22
  615.2 11.7 %cholesky.204 = f32[128,128]{1,0:T(8,128)S(1)} custom-call(f32[128,128]{1,0:T(8,128)S(1)} %fusion.19), custom_call_target="Cholesky" | custom-call | tf_op jit(solution)/shard_map/jit(cholesky)/cholesky | solution.py:24
  628.8 9.8 custom-call.18
  638.7 2.3 fusion.3
  641.9 2.8 convolution_subtract_fusion.2
  650.6 118.5 %all-gather.26.cloned.1.call-done = f32[2048,2048]{0,1:T(8,128)} async-done(((f32[128,2048]{0,1:T(8,128)}), f32[2048,2048]{0,1:T(8,128)}) %all-gather.26.cloned.1.call-update) | async-done | bytes 16777232 | tf_op jit(solution)/shard_map/all_gather | solution.py:55
  769.2 17.6 %copy.31 = f32[2048,2048]{1,0:T(8,128)} copy(f32[2048,2048]{0,1:T(8,128)} %all-gather.26.cloned.1.call-done) | data formatting | bytes 33554432 | tf_op jit(solution)/shard_map/all_gather | solution.py:55
  786.8 7.3 gather_fusion.1
  796.5 1.4 copy.32
  797.9 1.3 bitcast_add_fusion
  799.3 1.6 collective-permute-start.2
  800.9 22.0 %collective-permute-done.2 = f32[128,2048]{0,1:T(8,128)S(1)} collective-permute-done((f32[128,2048]{0,1:T(8,128)S(1)}, f32[128,2048]{0,1:T(8,128)S(1)}, u32[]{:S(2)}, u32[]{:S(2)}) %collective-permute-start.2) | collective-permute-done | bytes 1048608 | tf_op jit(solution)/shard_map/ppermute | solution.py:14
  823.7 47.7 %all-gather.28.cloned.1.call-done = f32[2048,128]{0,1:T(8,128)} async-done(((f32[128,128]{0,1:T(8,128)}), f32[2048,128]{0,1:T(8,128)}) %all-gather.28.cloned.1.call-update) | async-done | bytes 1048592 | tf_op jit(solution)/shard_map/all_gather | solution.py:22
  871.4 1.5 slice.252
  872.9 1.6 copy.35
  874.4 1.5 fusion.17
  875.9 13.2 %cholesky.215 = f32[128,128]{1,0:T(8,128)} custom-call(f32[128,128]{1,0:T(8,128)} %fusion.17), custom_call_target="Cholesky" | custom-call | tf_op jit(solution)/shard_map/jit(cholesky)/cholesky | solution.py:24
  890.6 2.2 select_bitcast_fusion.2
  892.8 11.3 %custom-call.19 = f32[1,128,128]{1,2,0:T(8,128)} custom-call(f32[1,128,128]{2,1,0:T(8,128)} %get-tuple-element.123), custom_call_target="InvertDiagBlocksLowerTriangular" | custom-call | tf_op jit(solution)/shard_map/triangular_solve/custom-call.0 | solution.py:25
  904.1 2.3 fusion.2
  906.4 1.8 convolution_subtract_fusion.1
  910.9 46.7 %all-gather.30.cloned.1.call-done = f32[2048,128]{0,1:T(8,128)} async-done(((f32[128,128]{0,1:T(8,128)}), f32[2048,128]{0,1:T(8,128)}) %all-gather.30.cloned.1.call-update) | async-done | bytes 1048592 | tf_op jit(solution)/shard_map/all_gather | solution.py:22
  959.4 11.7 %cholesky.226 = f32[128,128]{1,0:T(8,128)S(1)} custom-call(f32[128,128]{1,0:T(8,128)S(1)} %fusion.15), custom_call_target="Cholesky" | custom-call | tf_op jit(solution)/shard_map/jit(cholesky)/cholesky | solution.py:24
  972.5 10.4 custom-call.20
  982.9 2.3 fusion.1
  985.2 3.0 convolution_subtract_fusion
  1003.0 34.7 %all-gather.32.cloned.1.call-done = f32[2048,128]{0,1:T(8,128)} async-done(((f32[128,128]{0,1:T(8,128)}), f32[2048,128]{0,1:T(8,128)}) %all-gather.32.cloned.1.call-update) | async-done | bytes 1048592 | tf_op jit(solution)/shard_map/all_gather | solution.py:22
  1039.4 11.9 %cholesky.237 = f32[128,128]{1,0:T(8,128)S(1)} custom-call(f32[128,128]{1,0:T(8,128)S(1)} %fusion.13), custom_call_target="Cholesky" | custom-call | tf_op jit(solution)/shard_map/jit(cholesky)/cholesky | solution.py:24
  1052.7 9.8 custom-call.21
  1062.5 2.3 fusion
  1064.8 1.8 fusion.31
  1067.6 1.3 fusion.11
  (172 shorter events, 74.6 us)
Async XLA Ops:
  7.2 639.0 %copy-start = (s32[8,13]{1,0:T(8,128)S(1)}, s32[8,13]{1,0:T(8,128)}, u32[]{:S(2)}) copy-start(s32[8,13]{1,0:T(8,128)} %param.32) | copy-start | bytes 1252
  7.2 242.1 %copy-start.13 = (s32[1,13]{1,0:T(1,128)S(1)}, s32[1,13]{1,0:T(1,128)}, u32[]{:S(2)}) copy-start(s32[1,13]{1,0:T(1,128)} %param.31) | copy-start | bytes 160
  7.2 54.6 %all-gather.12.cloned.1.call-start = ((), (), s32[]{:S(2)}) async-start(), calls=%async_computation | async-start | bytes 1114112 | tf_op jit(solution)/shard_map/all_gather | solution.py:22
  9.2 129.7 %all-gather.14.cloned.1.call-start = ((), (), s32[]{:S(2)}) async-start(), calls=%async_computation.1 | async-start | bytes 1114112 | tf_op jit(solution)/shard_map/all_gather | solution.py:22
  91.2 125.8 %all-gather.16.cloned.1.call-start = ((), (), s32[]{:S(2)}) async-start(), calls=%async_computation.2 | async-start | bytes 1114112 | tf_op jit(solution)/shard_map/all_gather | solution.py:22
  167.7 1.0 copy-start.7
  169.3 204.1 %all-gather.18.cloned.1.call-start = ((), (), s32[]{:S(2)}) async-start(), calls=%async_computation.3 | async-start | bytes 17825792 | tf_op jit(solution)/shard_map/all_gather | solution.py:55
  243.9 1.0 copy-start.1
  249.0 205.7 %all-gather.20.cloned.1.call-start = ((), (), s32[]{:S(2)}) async-start(), calls=%async_computation.4 | async-start | bytes 1114112 | tf_op jit(solution)/shard_map/all_gather | solution.py:22
  403.5 2.7 collective-permute-start
  407.0 126.4 %all-gather.22.cloned.1.call-start = ((), (), s32[]{:S(2)}) async-start(), calls=%async_computation.5 | async-start | bytes 1114112 | tf_op jit(solution)/shard_map/all_gather | solution.py:22
  482.2 1.8 copy-start.2
  484.1 1.0 copy-start.8
  485.7 127.6 %all-gather.24.cloned.1.call-start = ((), (), s32[]{:S(2)}) async-start(), calls=%async_computation.6 | async-start | bytes 1114112 | tf_op jit(solution)/shard_map/all_gather | solution.py:22
  561.0 1.0 copy-start.3
  565.7 203.5 %all-gather.26.cloned.1.call-start = ((), (), s32[]{:S(2)}) async-start(), calls=%async_computation.7 | async-start | bytes 17825792 | tf_op jit(solution)/shard_map/all_gather | solution.py:55
  640.9 1.0 copy-start.4
  644.8 226.6 %all-gather.28.cloned.1.call-start = ((), (), s32[]{:S(2)}) async-start(), calls=%async_computation.8 | async-start | bytes 1114112 | tf_op jit(solution)/shard_map/all_gather | solution.py:22
  645.9 4.7 collective-permute-start.1
  799.2 195.6 %copy-start.10 = (f32[128,128]{1,0:T(8,128)S(1)}, f32[128,128]{1,0:T(8,128)}, u32[]{:S(2)}) copy-start(f32[128,128]{1,0:T(8,128)} %get-tuple-element.130) | copy-start | bytes 196612
  799.3 197.1 %copy-start.11 = (f32[128,128]{1,0:T(8,128)S(1)}, f32[128,128]{1,0:T(8,128)}, u32[]{:S(2)}) copy-start(f32[128,128]{1,0:T(8,128)} %get-tuple-element.128) | copy-start | bytes 196612
  799.3 198.7 %copy-start.12 = (f32[128,128]{1,0:T(8,128)S(1)}, f32[128,128]{1,0:T(8,128)}, u32[]{:S(2)}) copy-start(f32[128,128]{1,0:T(8,128)} %get-tuple-element.126) | copy-start | bytes 196612
  799.3 23.6 %collective-permute-start.2 = (f32[128,2048]{0,1:T(8,128)S(1)}, f32[128,2048]{0,1:T(8,128)S(1)}, u32[]{:S(2)}, u32[]{:S(2)}) collective-permute-start(f32[128,2048]{0,1:T(8,128)S(1)} %bitcast_add_fusion), channel_id=1, source_target_pairs={{0,32},{16,48},{32,0},{48,16},{64,96},{80,112},{96,64},{112,80},{1... | collective-permute-start | bytes 3145736 | tf_op jit(solution)/shard_map/ppermute | solution.py:14
  823.7 133.9 %all-gather.30.cloned.1.call-start = ((), (), s32[]{:S(2)}) async-start(), calls=%async_computation.9 | async-start | bytes 1114112 | tf_op jit(solution)/shard_map/all_gather | solution.py:22
  906.4 1.8 copy-start.5
  908.2 1.0 copy-start.6
  909.9 127.7 %all-gather.32.cloned.1.call-start = ((), (), s32[]{:S(2)}) async-start(), calls=%async_computation.10 | async-start | bytes 1114112 | tf_op jit(solution)/shard_map/all_gather | solution.py:22
  988.2 1.0 copy-start.9
Sparse Core Ops, SparseCore 0:
  11.0 50.7 all-gather.11
  91.3 47.5 all-gather.13
  169.4 47.5 all-gather.15
  249.1 124.2 all-gather.17
  407.1 47.5 all-gather.19
  485.9 47.5 all-gather.21
  565.8 47.5 all-gather.23
  644.9 124.2 all-gather.25
  823.8 47.5 all-gather.27
  910.0 47.5 all-gather.29
  990.1 47.5 all-gather.31
where the time goes:
time: 1090 us; the launch traced here: 1080 us
  waiting for transfers between devices  680 us (62%)
  other arithmetic  237 us (22%)
  local copies, waits for them, and re-layouts  94.7 us (9%)
  matrix products  44.9 us (4%)
  between operations  16.4 us (2%)
    all_gather x9, waiting for transfers between devices, eliminate(): lax.all_gather(front[:, block_low:block_low + BLK], 'fr', axis=0, tiled=T...  419 us
    all_gather x2, waiting for transfers between devices, extend(): shard_rows = lax.all_gather(front, 'fr', axis=0, tiled=True)  237 us
    another operation x27, other arithmetic, eliminate(): lower_block = jnp.linalg.cholesky(gathered[block_low:block_low + BLK])  114 us
    another operation x18, other arithmetic, eliminate(): lax.linalg.triangular_solve(lower_block, gathered, left_side=False, lower...  99.7 us
    all_gather x2, local copies, waits for them, and re-layouts, extend(): shard_rows = lax.all_gather(front, 'fr', axis=0, tiled=True)  35.2 us
    ppermute x3, waiting for transfers between devices, partner(): lax.ppermute(array, axis, [(i, i ^ 1 << stride) for i in range(lax.axis_s...  24.6 us
    dot_general x9, matrix products, eliminate(): jnp.dot(own_below, below.T, precision=HIGH, preferred_element_type=jnp.fl...  22 us
  transfers between devices with their start and end apart: 14, of which 13 were waited for; matrix products, arithmetic and copies ran while one was open for 2% of the time, Pallas kernels for 0%

commit v1 on v0

--- a/solution.py
+++ b/solution.py
@@ -52,7 +52,19 @@
     source_block = jnp.sum(jnp.where(matches, jnp.arange(NFB)[None, :], 0), axis=1)
     source_rows = (source_block[:, None] * BLK + jnp.arange(BLK)[None, :]).reshape(row_count)
     is_live = jnp.repeat(present, BLK)
-    shard_rows = lax.all_gather(front, "fr", axis=0, tiled=True)
+    ways, here, lap = (lax.axis_size("fr"), lax.axis_index("fr"), front.shape[0])
+    dims = [n * ways if d == 0 else n for d, n in enumerate(front.shape)]
+    full = lax.dynamic_update_slice_in_dim(jnp.zeros(dims, front.dtype), front, here * lap, axis=0)
+    going_up = going_down = front
+    for far in range(1, ways // 2 + 1):
+        going_up = lax.ppermute(going_up, "fr", [(d, (d + 1) % ways) for d in range(ways)])
+        full = lax.dynamic_update_slice_in_dim(full, going_up, (here - far) % ways * lap, axis=0)
+        if 2 * far < ways:
+            going_down = lax.ppermute(going_down, "fr", [(d, (d - 1) % ways) for d in range(ways)])
+            full = lax.dynamic_update_slice_in_dim(
+                full, going_down, (here + far) % ways * lap, axis=0
+            )
+    shard_rows = full
     inside = is_live & (source_rows >= 0) & (source_rows < shard_rows.shape[0])
     picked_rows = jnp.take(shard_rows, jnp.clip(source_rows, 0, shard_rows.shape[0] - 1), axis=0)
     picked_rows = jnp.where(inside[:, None], picked_rows, 0.0)

time: 1090 us -> 1200 us (1.10)
  local copies, waits for them, and re-layouts: 94.7 us -> 182 us
  starting transfers between devices: 4.07 us -> 65.1 us
  waiting for transfers between devices: 680 us -> 640 us
    all_gather x2 -> x0, waiting for transfers between devices: 237 us -> none  [extend(): shard_rows = lax.all_gather(front, 'fr', axis=0, tiled=True)]
    ppermute x0 -> x30, waiting for transfers between devices: none -> 201 us  [the longest x16 194 us: extend(): lax.ppermute(going_up, 'fr', [(d, (d + 1) % ways) for d in range(ways)])]
    ppermute x0 -> x30, starting transfers between devices: none -> 61 us  [the longest x14 59.2 us: extend(): lax.ppermute(going_down, 'fr', [(d, (d - 1) % ways) for d in range(ways)])]
    ppermute x0 -> x30, local copies, waits for them, and re-layouts: none -> 56.8 us  [the longest x16 31 us: extend(): lax.ppermute(going_up, 'fr', [(d, (d + 1) % ways) for d in range(ways)])]
    dynamic_update_slice x0 -> x32, local copies, waits for them, and re-layouts: none -> 46.8 us  [the longest x16 24.6 us: extend(): lax.dynamic_update_slice_in_dim(full, going_up, (here - far) % ways * lap...]
    all_gather x2 -> x0, local copies, waits for them, and re-layouts: 35.2 us -> none  [extend(): shard_rows = lax.all_gather(front, 'fr', axis=0, tiled=True)]
    another operation x0 -> x2, local copies, waits for them, and re-layouts: none -> 15.8 us
  transfers between devices with their start and end apart: 14 -> 42, of which waited for: 13 -> 27; matrix products, arithmetic and copies ran while one was open for 2% -> 12% of each run, Pallas kernels for 0% -> 0%
where the time goes in v1:
time: 1200 us; the launch traced here: 1180 us
  waiting for transfers between devices  640 us (53%)
  other arithmetic  238 us (20%)
  local copies, waits for them, and re-layouts  182 us (15%)
  starting transfers between devices  65.1 us (5%)
  matrix products  42.3 us (4%)
  between operations  17.1 us (1%)
    all_gather x9, waiting for transfers between devices, eliminate(): lax.all_gather(front[:, block_low:block_low + BLK], 'fr', axis=0, tiled=T...  422 us
    ppermute x16, waiting for transfers between devices, extend(): lax.ppermute(going_up, 'fr', [(d, (d + 1) % ways) for d in range(ways)])  194 us
    another operation x27, other arithmetic, eliminate(): lower_block = jnp.linalg.cholesky(gathered[block_low:block_low + BLK])  114 us
    another operation x18, other arithmetic, eliminate(): lax.linalg.triangular_solve(lower_block, gathered, left_side=False, lower...  101 us
    ppermute x14, starting transfers between devices, extend(): lax.ppermute(going_down, 'fr', [(d, (d - 1) % ways) for d in range(ways)])  59.2 us
    ppermute x16, local copies, waits for them, and re-layouts, extend(): lax.ppermute(going_up, 'fr', [(d, (d + 1) % ways) for d in range(ways)])  31 us
    ppermute x14, local copies, waits for them, and re-layouts, extend(): lax.ppermute(going_down, 'fr', [(d, (d - 1) % ways) for d in range(ways)])  25.8 us
    dynamic_update_slice x16, local copies, waits for them, and re-layouts, extend(): lax.dynamic_update_slice_in_dim(full, going_up, (here - far) % ways * lap...  24.6 us
  transfers between devices with their start and end apart: 42, of which 27 were waited for; matrix products, arithmetic and copies ran while one was open for 12% of the time, Pallas kernels for 0%

profile of v1, /device:TPU:2, one launch (start us, length us, event | category | flops | bytes accessed | tf_op | source)
XLA Modules:
  0.0 1184.9 jit_solution(18114673090374898388)
XLA Ops:
  9.3 52.5 %all-gather.10.cloned.1.call-done = f32[2048,128]{0,1:T(8,128)} async-done(((f32[128,128]{0,1:T(8,128)}), f32[2048,128]{0,1:T(8,128)}) %all-gather.10.cloned.1.call-update) | async-done | bytes 1048592 | tf_op jit(solution)/shard_map/all_gather | solution.py:22
  63.6 11.7 cholesky.149
  77.3 9.8 custom-call.13
  92.1 47.4 %all-gather.12.cloned.1.call-done = f32[2048,128]{0,1:T(8,128)} async-done(((f32[128,128]{0,1:T(8,128)}), f32[2048,128]{0,1:T(8,128)}) %all-gather.12.cloned.1.call-update) | async-done | bytes 1048592 | tf_op jit(solution)/shard_map/all_gather | solution.py:22
  141.3 11.7 cholesky.160
  155.0 9.8 custom-call.14
  171.0 47.2 %all-gather.14.cloned.1.call-done = f32[2048,128]{0,1:T(8,128)} async-done(((f32[128,128]{0,1:T(8,128)}), f32[2048,128]{0,1:T(8,128)}) %all-gather.14.cloned.1.call-update) | async-done | bytes 1048592 | tf_op jit(solution)/shard_map/all_gather | solution.py:22
  220.0 11.7 cholesky.171
  233.7 9.8 custom-call.15
  246.8 3.0 convolution_subtract_fusion.5
  251.9 21.3 %collective-permute-done = f32[128,2048]{0,1:T(8,128)S(1)} collective-permute-done((f32[128,2048]{0,1:T(8,128)S(1)}, f32[128,2048]{0,1:T(8,128)S(1)}, u32[]{:S(2)}, u32[]{:S(2)}) %collective-permute-start) | collective-permute-done | bytes 1048608 | tf_op jit(solution)/shard_map/ppermute | solution.py:60
  274.1 3.3 collective-permute-start.3
  277.5 20.6 %collective-permute-done.2 = f32[128,2048]{0,1:T(8,128)S(1)} collective-permute-done((f32[128,2048]{0,1:T(8,128)S(1)}, f32[128,2048]{0,1:T(8,128)S(1)}, u32[]{:S(2)}, u32[]{:S(2)}) %collective-permute-start.2) | collective-permute-done | bytes 1048608 | tf_op jit(solution)/shard_map/ppermute | solution.py:60
  298.2 5.1 collective-permute-start.5
  303.4 19.7 %collective-permute-done.4 = f32[128,2048]{0,1:T(8,128)S(1)} collective-permute-done((f32[128,2048]{0,1:T(8,128)S(1)}, f32[128,2048]{0,1:T(8,128)S(1)}, u32[]{:S(2)}, u32[]{:S(2)}) %collective-permute-start.4) | collective-permute-done | bytes 1048608 | tf_op jit(solution)/shard_map/ppermute | solution.py:60
  323.1 5.1 collective-permute-start.7
  328.3 19.0 %collective-permute-done.6 = f32[128,2048]{0,1:T(8,128)} collective-permute-done((f32[128,2048]{0,1:T(8,128)S(1)}, f32[128,2048]{0,1:T(8,128)}, u32[]{:S(2)}, u32[]{:S(2)}) %collective-permute-start.6) | collective-permute-done | bytes 1048608 | tf_op jit(solution)/shard_map/ppermute | solution.py:60
  351.1 5.1 collective-permute-start.9
  358.3 12.4 %collective-permute-done.8 = f32[128,2048]{0,1:T(8,128)} collective-permute-done((f32[128,2048]{0,1:T(8,128)}, f32[128,2048]{0,1:T(8,128)}, u32[]{:S(2)}, u32[]{:S(2)}) %collective-permute-start.8) | collective-permute-done | bytes 1048608 | tf_op jit(solution)/shard_map/ppermute | solution.py:60
  370.7 7.9 broadcast.263.clone
  388.7 5.1 collective-permute-start.11
  409.4 2.8 collective-permute-done.11
  412.2 4.5 collective-permute-start.13
  417.8 2.6 copy.28
  440.5 5.1 collective-permute-done.14
  448.2 7.2 gather_fusion
  459.3 2.6 collective-permute-done.15
  463.0 49.2 %all-gather.16.cloned.1.call-done = f32[2048,128]{0,1:T(8,128)} async-done(((f32[128,128]{0,1:T(8,128)}), f32[2048,128]{0,1:T(8,128)}) %all-gather.16.cloned.1.call-update) | async-done | bytes 1048592 | tf_op jit(solution)/shard_map/all_gather | solution.py:22
  514.0 11.7 cholesky.182
  527.8 9.8 custom-call.16
  543.8 47.2 %all-gather.18.cloned.1.call-done = f32[2048,128]{0,1:T(8,128)} async-done(((f32[128,128]{0,1:T(8,128)}), f32[2048,128]{0,1:T(8,128)}) %all-gather.18.cloned.1.call-update) | async-done | bytes 1048592 | tf_op jit(solution)/shard_map/all_gather | solution.py:22
  592.8 11.7 cholesky.193
  606.4 9.8 custom-call.17
  619.5 3.0 convolution_subtract_fusion.3
  623.4 47.5 %all-gather.20.cloned.1.call-done = f32[2048,128]{0,1:T(8,128)} async-done(((f32[128,128]{0,1:T(8,128)}), f32[2048,128]{0,1:T(8,128)}) %all-gather.20.cloned.1.call-update) | async-done | bytes 1048592 | tf_op jit(solution)/shard_map/all_gather | solution.py:22
  672.7 11.7 cholesky.204
  686.4 9.8 custom-call.18
  703.4 21.3 %collective-permute-done.16 = f32[128,2048]{0,1:T(8,128)S(1)} collective-permute-done((f32[128,2048]{0,1:T(8,128)S(1)}, f32[128,2048]{0,1:T(8,128)S(1)}, u32[]{:S(2)}, u32[]{:S(2)}) %collective-permute-start.16) | collective-permute-done | bytes 1048608 | tf_op jit(solution)/shard_map/ppermute | solution.py:60
  725.6 3.3 collective-permute-start.19
  728.9 20.6 %collective-permute-done.18 = f32[128,2048]{0,1:T(8,128)S(1)} collective-permute-done((f32[128,2048]{0,1:T(8,128)S(1)}, f32[128,2048]{0,1:T(8,128)S(1)}, u32[]{:S(2)}, u32[]{:S(2)}) %collective-permute-start.18) | collective-permute-done | bytes 1048608 | tf_op jit(solution)/shard_map/ppermute | solution.py:60
  749.7 5.1 collective-permute-start.21
  754.9 19.7 %collective-permute-done.20 = f32[128,2048]{0,1:T(8,128)S(1)} collective-permute-done((f32[128,2048]{0,1:T(8,128)S(1)}, f32[128,2048]{0,1:T(8,128)S(1)}, u32[]{:S(2)}, u32[]{:S(2)}) %collective-permute-start.20) | collective-permute-done | bytes 1048608 | tf_op jit(solution)/shard_map/ppermute | solution.py:60
  774.6 5.1 collective-permute-start.23
  779.7 19.0 %collective-permute-done.22 = f32[128,2048]{0,1:T(8,128)} collective-permute-done((f32[128,2048]{0,1:T(8,128)S(1)}, f32[128,2048]{0,1:T(8,128)}, u32[]{:S(2)}, u32[]{:S(2)}) %collective-permute-start.22) | collective-permute-done | bytes 1048608 | tf_op jit(solution)/shard_map/ppermute | solution.py:60
  802.6 5.1 collective-permute-start.25
  812.0 10.2 collective-permute-done.24
  822.2 7.9 broadcast.263
  840.2 5.1 collective-permute-start.27
  860.9 2.6 collective-permute-done.27
  863.5 4.7 collective-permute-start.29
  869.3 2.6 copy.55
  892.0 5.3 collective-permute-done.30
  899.9 7.4 gather_fusion.1
  914.2 14.8 %collective-permute-done.32 = f32[128,2048]{0,1:T(8,128)S(1)} collective-permute-done((f32[128,2048]{0,1:T(8,128)S(1)}, f32[128,2048]{0,1:T(8,128)S(1)}, u32[]{:S(2)}, u32[]{:S(2)}) %collective-permute-start.32) | collective-permute-done | bytes 1048608 | tf_op jit(solution)/shard_map/ppermute | solution.py:14
  929.9 49.4 %all-gather.22.cloned.1.call-done = f32[2048,128]{0,1:T(8,128)} async-done(((f32[128,128]{0,1:T(8,128)}), f32[2048,128]{0,1:T(8,128)}) %all-gather.22.cloned.1.call-update) | async-done | bytes 1048592 | tf_op jit(solution)/shard_map/all_gather | solution.py:22
  983.9 13.2 %cholesky.215 = f32[128,128]{1,0:T(8,128)} custom-call(f32[128,128]{1,0:T(8,128)} %fusion.17), custom_call_target="Cholesky" | custom-call | tf_op jit(solution)/shard_map/jit(cholesky)/cholesky | solution.py:24
  1000.8 11.3 custom-call.19
  1018.8 46.7 %all-gather.24.cloned.1.call-done = f32[2048,128]{0,1:T(8,128)} async-done(((f32[128,128]{0,1:T(8,128)}), f32[2048,128]{0,1:T(8,128)}) %all-gather.24.cloned.1.call-update) | async-done | bytes 1048592 | tf_op jit(solution)/shard_map/all_gather | solution.py:22
  1067.3 11.7 cholesky.226
  1080.3 10.4 custom-call.20
  1093.0 3.0 convolution_subtract_fusion
  1110.8 34.6 %all-gather.26.cloned.1.call-done = f32[2048,128]{0,1:T(8,128)} async-done(((f32[128,128]{0,1:T(8,128)}), f32[2048,128]{0,1:T(8,128)}) %all-gather.26.cloned.1.call-update) | async-done | bytes 1048592 | tf_op jit(solution)/shard_map/all_gather | solution.py:22
  1147.2 12.0 %cholesky.237 = f32[128,128]{1,0:T(8,128)S(1)} custom-call(f32[128,128]{1,0:T(8,128)S(1)} %fusion.13), custom_call_target="Cholesky" | custom-call | tf_op jit(solution)/shard_map/jit(cholesky)/cholesky | solution.py:24
  1160.5 9.8 custom-call.21
  (328 shorter events, 230.1 us)
Async XLA Ops:
  7.2 792.7 %copy-start = (s32[8,13]{1,0:T(8,128)S(1)}, s32[8,13]{1,0:T(8,128)}, u32[]{:S(2)}) copy-start(s32[8,13]{1,0:T(8,128)} %param.32) | copy-start | bytes 1252
  7.2 340.3 %copy-start.32 = (s32[1,13]{1,0:T(1,128)S(1)}, s32[1,13]{1,0:T(1,128)}, u32[]{:S(2)}) copy-start(s32[1,13]{1,0:T(1,128)} %param.31) | copy-start | bytes 160
  7.2 342.2 %copy-start.30 = (f32[128,384]{1,0:T(8,128)S(1)}, f32[128,384]{1,0:T(8,128)}, u32[]{:S(2)}) copy-start(f32[128,384]{1,0:T(8,128)} %param.29) | copy-start | bytes 589828
  7.2 54.6 %all-gather.10.cloned.1.call-start = ((), (), s32[]{:S(2)}) async-start(), calls=%async_computation | async-start | bytes 1114112 | tf_op jit(solution)/shard_map/all_gather | solution.py:22
  9.3 130.3 %all-gather.12.cloned.1.call-start = ((), (), s32[]{:S(2)}) async-start(), calls=%async_computation.1 | async-start | bytes 1114112 | tf_op jit(solution)/shard_map/all_gather | solution.py:22
  91.8 126.4 %all-gather.14.cloned.1.call-start = ((), (), s32[]{:S(2)}) async-start(), calls=%async_computation.2 | async-start | bytes 1114112 | tf_op jit(solution)/shard_map/all_gather | solution.py:22
  170.5 341.7 %all-gather.16.cloned.1.call-start = ((), (), s32[]{:S(2)}) async-start(), calls=%async_computation.3 | async-start | bytes 1114112 | tf_op jit(solution)/shard_map/all_gather | solution.py:22
  249.8 23.4 %collective-permute-start = (f32[128,2048]{0,1:T(8,128)S(1)}, f32[128,2048]{0,1:T(8,128)S(1)}, u32[]{:S(2)}, u32[]{:S(2)}) collective-permute-start(f32[128,2048]{0,1:T(8,128)S(1)} %convolution_subtract_fusion.5), channel_id=1, source_target_pairs={{0,1},{1,2},{2,3},{3,4},{4,5},{5,6},{6,7},{7,8},{8,9},{9,10},{10,1... | collective-permute-start | bytes 3145736 | tf_op jit(solution)/shard_map/ppermute | solution.py:60
  250.8 23.3 %collective-permute-start.1 = (f32[128,2048]{0,1:T(8,128)S(1)}, f32[128,2048]{0,1:T(8,128)S(1)}, u32[]{:S(2)}, u32[]{:S(2)}) collective-permute-start(f32[128,2048]{0,1:T(8,128)S(1)} %convolution_subtract_fusion.5), channel_id=1, source_target_pairs={{0,15},{1,0},{2,1},{3,2},{4,3},{5,4},{6,5},{7,6},{8,7},{9,8},{10,9... | collective-permute-start | bytes 3145736 | tf_op jit(solution)/shard_map/ppermute | solution.py:63
  273.2 4.3 copy-start.15
  273.2 24.9 %collective-permute-start.2 = (f32[128,2048]{0,1:T(8,128)S(1)}, f32[128,2048]{0,1:T(8,128)S(1)}, u32[]{:S(2)}, u32[]{:S(2)}) collective-permute-start(f32[128,2048]{0,1:T(8,128)S(1)} %collective-permute-done), channel_id=1, source_target_pairs={{0,1},{1,2},{2,3},{3,4},{4,5},{5,6},{6,7},{7,8},{8,9},{9,10},{10,1... | collective-permute-start | bytes 3145736 | tf_op jit(solution)/shard_map/ppermute | solution.py:60
  274.1 73.1 %copy-start.17 = (f32[128,2048]{0,1:T(8,128)}, f32[128,2048]{0,1:T(8,128)S(1)}, u32[]{:S(2)}) copy-start(f32[128,2048]{0,1:T(8,128)S(1)} %collective-permute-done.1) | copy-start | bytes 3145732
  274.1 24.1 %collective-permute-start.3 = (f32[128,2048]{0,1:T(8,128)S(1)}, f32[128,2048]{0,1:T(8,128)S(1)}, u32[]{:S(2)}, u32[]{:S(2)}) collective-permute-start(f32[128,2048]{0,1:T(8,128)S(1)} %collective-permute-done.1), channel_id=1, source_target_pairs={{0,15},{1,0},{2,1},{3,2},{4,3},{5,4},{6,5},{7,6},{8,7},{9,8},{10,9... | collective-permute-start | bytes 3145736 | tf_op jit(solution)/shard_map/ppermute | solution.py:63
  298.0 49.2 %copy-start.16 = (f32[128,2048]{0,1:T(8,128)}, f32[128,2048]{0,1:T(8,128)S(1)}, u32[]{:S(2)}) copy-start(f32[128,2048]{0,1:T(8,128)S(1)} %collective-permute-done.2) | copy-start | bytes 3145732
  298.0 25.0 %collective-permute-start.4 = (f32[128,2048]{0,1:T(8,128)S(1)}, f32[128,2048]{0,1:T(8,128)S(1)}, u32[]{:S(2)}, u32[]{:S(2)}) collective-permute-start(f32[128,2048]{0,1:T(8,128)S(1)} %collective-permute-done.2), channel_id=1, source_target_pairs={{0,1},{1,2},{2,3},{3,4},{4,5},{5,6},{6,7},{7,8},{8,9},{9,10},{10,1... | collective-permute-start | bytes 3145736 | tf_op jit(solution)/shard_map/ppermute | solution.py:60
  298.2 24.9 %copy-start.13 = (f32[128,2048]{0,1:T(8,128)}, f32[128,2048]{0,1:T(8,128)S(1)}, u32[]{:S(2)}) copy-start(f32[128,2048]{0,1:T(8,128)S(1)} %collective-permute-done.3) | copy-start | bytes 3145732
  298.2 24.9 %collective-permute-start.5 = (f32[128,2048]{0,1:T(8,128)S(1)}, f32[128,2048]{0,1:T(8,128)S(1)}, u32[]{:S(2)}, u32[]{:S(2)}) collective-permute-start(f32[128,2048]{0,1:T(8,128)S(1)} %collective-permute-done.3), channel_id=1, source_target_pairs={{0,15},{1,0},{2,1},{3,2},{4,3},{5,4},{6,5},{7,6},{8,7},{9,8},{10,9... | collective-permute-start | bytes 3145736 | tf_op jit(solution)/shard_map/ppermute | solution.py:63
  323.1 5.2 copy-start.14
  323.1 24.1 %collective-permute-start.6 = (f32[128,2048]{0,1:T(8,128)S(1)}, f32[128,2048]{0,1:T(8,128)}, u32[]{:S(2)}, u32[]{:S(2)}) collective-permute-start(f32[128,2048]{0,1:T(8,128)S(1)} %collective-permute-done.4), channel_id=1, source_target_pairs={{0,1},{1,2},{2,3},{3,4},{4,5},{5,6},{6,7},{7,8},{8,9},{9,10},{10,1... | collective-permute-start | bytes 3145736 | tf_op jit(solution)/shard_map/ppermute | solution.py:60
  323.1 33.6 %copy-start.12 = (f32[128,2048]{0,1:T(8,128)}, f32[128,2048]{0,1:T(8,128)S(1)}, u32[]{:S(2)}) copy-start(f32[128,2048]{0,1:T(8,128)S(1)} %collective-permute-done.5) | copy-start | bytes 3145732
  323.1 27.9 %collective-permute-start.7 = (f32[128,2048]{0,1:T(8,128)S(1)}, f32[128,2048]{0,1:T(8,128)}, u32[]{:S(2)}, u32[]{:S(2)}) collective-permute-start(f32[128,2048]{0,1:T(8,128)S(1)} %collective-permute-done.5), channel_id=1, source_target_pairs={{0,15},{1,0},{2,1},{3,2},{4,3},{5,4},{6,5},{7,6},{8,7},{9,8},{10,9... | collective-permute-start | bytes 3145736 | tf_op jit(solution)/shard_map/ppermute | solution.py:63
  347.2 23.5 %collective-permute-start.8 = (f32[128,2048]{0,1:T(8,128)}, f32[128,2048]{0,1:T(8,128)}, u32[]{:S(2)}, u32[]{:S(2)}) collective-permute-start(f32[128,2048]{0,1:T(8,128)} %collective-permute-done.6), channel_id=1, source_target_pairs={{0,1},{1,2},{2,3},{3,4},{4,5},{5,6},{6,7},{7,8},{8,9},{9,10},{10,1... | collective-permute-start | bytes 3145736 | tf_op jit(solution)/shard_map/ppermute | solution.py:60
  351.1 37.7 %collective-permute-start.9 = (f32[128,2048]{0,1:T(8,128)}, f32[128,2048]{0,1:T(8,128)}, u32[]{:S(2)}, u32[]{:S(2)}) collective-permute-start(f32[128,2048]{0,1:T(8,128)} %collective-permute-done.7), channel_id=1, source_target_pairs={{0,15},{1,0},{2,1},{3,2},{4,3},{5,4},{6,5},{7,6},{8,7},{9,8},{10,9... | collective-permute-start | bytes 3145736 | tf_op jit(solution)/shard_map/ppermute | solution.py:63
  370.7 28.4 %collective-permute-start.10 = (f32[128,2048]{0,1:T(8,128)}, f32[128,2048]{0,1:T(8,128)}, u32[]{:S(2)}, u32[]{:S(2)}) collective-permute-start(f32[128,2048]{0,1:T(8,128)} %collective-permute-done.8), channel_id=1, source_target_pairs={{0,1},{1,2},{2,3},{3,4},{4,5},{5,6},{6,7},{7,8},{8,9},{9,10},{10,1... | collective-permute-start | bytes 3145736 | tf_op jit(solution)/shard_map/ppermute | solution.py:60
  388.7 23.5 %collective-permute-start.11 = (f32[128,2048]{0,1:T(8,128)}, f32[128,2048]{0,1:T(8,128)}, u32[]{:S(2)}, u32[]{:S(2)}) collective-permute-start(f32[128,2048]{0,1:T(8,128)} %collective-permute-done.9), channel_id=1, source_target_pairs={{0,15},{1,0},{2,1},{3,2},{4,3},{5,4},{6,5},{7,6},{8,7},{9,8},{10,9... | collective-permute-start | bytes 3145736 | tf_op jit(solution)/shard_map/ppermute | solution.py:63
  399.2 25.2 %collective-permute-start.12 = (f32[128,2048]{0,1:T(8,128)}, f32[128,2048]{0,1:T(8,128)}, u32[]{:S(2)}, u32[]{:S(2)}) collective-permute-start(f32[128,2048]{0,1:T(8,128)} %collective-permute-done.10), channel_id=1, source_target_pairs={{0,1},{1,2},{2,3},{3,4},{4,5},{5,6},{6,7},{7,8},{8,9},{9,10},{10,1... | collective-permute-start | bytes 3145736 | tf_op jit(solution)/shard_map/ppermute | solution.py:60
  412.2 22.3 %collective-permute-start.13 = (f32[128,2048]{0,1:T(8,128)}, f32[128,2048]{0,1:T(8,128)}, u32[]{:S(2)}, u32[]{:S(2)}) collective-permute-start(f32[128,2048]{0,1:T(8,128)} %collective-permute-done.11), channel_id=1, source_target_pairs={{0,15},{1,0},{2,1},{3,2},{4,3},{5,4},{6,5},{7,6},{8,7},{9,8},{10,9... | collective-permute-start | bytes 3145736 | tf_op jit(solution)/shard_map/ppermute | solution.py:63
  424.3 21.3 %collective-permute-start.14 = (f32[128,2048]{0,1:T(8,128)}, f32[128,2048]{0,1:T(8,128)}, u32[]{:S(2)}, u32[]{:S(2)}) collective-permute-start(f32[128,2048]{0,1:T(8,128)} %collective-permute-done.12), channel_id=1, source_target_pairs={{0,1},{1,2},{2,3},{3,4},{4,5},{5,6},{6,7},{7,8},{8,9},{9,10},{10,1... | collective-permute-start | bytes 3145736 | tf_op jit(solution)/shard_map/ppermute | solution.py:60
  427.0 28.9 %copy-start.31 = (s32[16]{0:T(128)S(1)}, s32[16]{0:T(128)}, u32[]{:S(2)}) copy-start(s32[16]{0:T(128)} %get-tuple-element.139) | copy-start | bytes 196
  459.2 2.7 collective-permute-start.15
  462.7 128.3 %all-gather.18.cloned.1.call-start = ((), (), s32[]{:S(2)}) async-start(), calls=%async_computation.4 | async-start | bytes 1114112 | tf_op jit(solution)/shard_map/all_gather | solution.py:22
  543.3 127.5 %all-gather.20.cloned.1.call-start = ((), (), s32[]{:S(2)}) async-start(), calls=%async_computation.5 | async-start | bytes 1114112 | tf_op jit(solution)/shard_map/all_gather | solution.py:22
  623.2 356.2 %all-gather.22.cloned.1.call-start = ((), (), s32[]{:S(2)}) async-start(), calls=%async_computation.6 | async-start | bytes 1114112 | tf_op jit(solution)/shard_map/all_gather | solution.py:22
  701.3 23.4 %collective-permute-start.16 = (f32[128,2048]{0,1:T(8,128)S(1)}, f32[128,2048]{0,1:T(8,128)S(1)}, u32[]{:S(2)}, u32[]{:S(2)}) collective-permute-start(f32[128,2048]{0,1:T(8,128)S(1)} %convolution_subtract_fusion.2), channel_id=1, source_target_pairs={{0,1},{1,2},{2,3},{3,4},{4,5},{5,6},{6,7},{7,8},{8,9},{9,10},{10,1... | collective-permute-start | bytes 3145736 | tf_op jit(solution)/shard_map/ppermute | solution.py:60
  702.3 23.3 %collective-permute-start.17 = (f32[128,2048]{0,1:T(8,128)S(1)}, f32[128,2048]{0,1:T(8,128)S(1)}, u32[]{:S(2)}, u32[]{:S(2)}) collective-permute-start(f32[128,2048]{0,1:T(8,128)S(1)} %convolution_subtract_fusion.2), channel_id=1, source_target_pairs={{0,15},{1,0},{2,1},{3,2},{4,3},{5,4},{6,5},{7,6},{8,7},{9,8},{10,9... | collective-permute-start | bytes 3145736 | tf_op jit(solution)/shard_map/ppermute | solution.py:63
  724.6 4.3 copy-start.22
  724.6 24.9 %collective-permute-start.18 = (f32[128,2048]{0,1:T(8,128)S(1)}, f32[128,2048]{0,1:T(8,128)S(1)}, u32[]{:S(2)}, u32[]{:S(2)}) collective-permute-start(f32[128,2048]{0,1:T(8,128)S(1)} %collective-permute-done.16), channel_id=1, source_target_pairs={{0,1},{1,2},{2,3},{3,4},{4,5},{5,6},{6,7},{7,8},{8,9},{9,10},{10,1... | collective-permute-start | bytes 3145736 | tf_op jit(solution)/shard_map/ppermute | solution.py:60
  725.6 73.1 %copy-start.23 = (f32[128,2048]{0,1:T(8,128)}, f32[128,2048]{0,1:T(8,128)S(1)}, u32[]{:S(2)}) copy-start(f32[128,2048]{0,1:T(8,128)S(1)} %collective-permute-done.17) | copy-start | bytes 3145732
  725.6 24.1 %collective-permute-start.19 = (f32[128,2048]{0,1:T(8,128)S(1)}, f32[128,2048]{0,1:T(8,128)S(1)}, u32[]{:S(2)}, u32[]{:S(2)}) collective-permute-start(f32[128,2048]{0,1:T(8,128)S(1)} %collective-permute-done.17), channel_id=1, source_target_pairs={{0,15},{1,0},{2,1},{3,2},{4,3},{5,4},{6,5},{7,6},{8,7},{9,8},{10,9... | collective-permute-start | bytes 3145736 | tf_op jit(solution)/shard_map/ppermute | solution.py:63
  749.5 49.2 %copy-start.21 = (f32[128,2048]{0,1:T(8,128)}, f32[128,2048]{0,1:T(8,128)S(1)}, u32[]{:S(2)}) copy-start(f32[128,2048]{0,1:T(8,128)S(1)} %collective-permute-done.18) | copy-start | bytes 3145732
  749.5 25.1 %collective-permute-start.20 = (f32[128,2048]{0,1:T(8,128)S(1)}, f32[128,2048]{0,1:T(8,128)S(1)}, u32[]{:S(2)}, u32[]{:S(2)}) collective-permute-start(f32[128,2048]{0,1:T(8,128)S(1)} %collective-permute-done.18), channel_id=1, source_target_pairs={{0,1},{1,2},{2,3},{3,4},{4,5},{5,6},{6,7},{7,8},{8,9},{9,10},{10,1... | collective-permute-start | bytes 3145736 | tf_op jit(solution)/shard_map/ppermute | solution.py:60
  749.7 24.9 %copy-start.19 = (f32[128,2048]{0,1:T(8,128)}, f32[128,2048]{0,1:T(8,128)S(1)}, u32[]{:S(2)}) copy-start(f32[128,2048]{0,1:T(8,128)S(1)} %collective-permute-done.19) | copy-start | bytes 3145732
  749.7 24.9 %collective-permute-start.21 = (f32[128,2048]{0,1:T(8,128)S(1)}, f32[128,2048]{0,1:T(8,128)S(1)}, u32[]{:S(2)}, u32[]{:S(2)}) collective-permute-start(f32[128,2048]{0,1:T(8,128)S(1)} %collective-permute-done.19), channel_id=1, source_target_pairs={{0,15},{1,0},{2,1},{3,2},{4,3},{5,4},{6,5},{7,6},{8,7},{9,8},{10,9... | collective-permute-start | bytes 3145736 | tf_op jit(solution)/shard_map/ppermute | solution.py:63
  774.6 5.2 copy-start.20
  774.6 24.1 %collective-permute-start.22 = (f32[128,2048]{0,1:T(8,128)S(1)}, f32[128,2048]{0,1:T(8,128)}, u32[]{:S(2)}, u32[]{:S(2)}) collective-permute-start(f32[128,2048]{0,1:T(8,128)S(1)} %collective-permute-done.20), channel_id=1, source_target_pairs={{0,1},{1,2},{2,3},{3,4},{4,5},{5,6},{6,7},{7,8},{8,9},{9,10},{10,1... | collective-permute-start | bytes 3145736 | tf_op jit(solution)/shard_map/ppermute | solution.py:60
  774.6 34.9 %copy-start.18 = (f32[128,2048]{0,1:T(8,128)}, f32[128,2048]{0,1:T(8,128)S(1)}, u32[]{:S(2)}) copy-start(f32[128,2048]{0,1:T(8,128)S(1)} %collective-permute-done.21) | copy-start | bytes 3145732
  774.6 28.0 %collective-permute-start.23 = (f32[128,2048]{0,1:T(8,128)S(1)}, f32[128,2048]{0,1:T(8,128)}, u32[]{:S(2)}, u32[]{:S(2)}) collective-permute-start(f32[128,2048]{0,1:T(8,128)S(1)} %collective-permute-done.21), channel_id=1, source_target_pairs={{0,15},{1,0},{2,1},{3,2},{4,3},{5,4},{6,5},{7,6},{8,7},{9,8},{10,9... | collective-permute-start | bytes 3145736 | tf_op jit(solution)/shard_map/ppermute | solution.py:63
  798.7 23.5 %collective-permute-start.24 = (f32[128,2048]{0,1:T(8,128)}, f32[128,2048]{0,1:T(8,128)}, u32[]{:S(2)}, u32[]{:S(2)}) collective-permute-start(f32[128,2048]{0,1:T(8,128)} %collective-permute-done.22), channel_id=1, source_target_pairs={{0,1},{1,2},{2,3},{3,4},{4,5},{5,6},{6,7},{7,8},{8,9},{9,10},{10,1... | collective-permute-start | bytes 3145736 | tf_op jit(solution)/shard_map/ppermute | solution.py:60
  799.8 9.7 collective-permute-start.31
  802.6 37.6 %collective-permute-start.25 = (f32[128,2048]{0,1:T(8,128)}, f32[128,2048]{0,1:T(8,128)}, u32[]{:S(2)}, u32[]{:S(2)}) collective-permute-start(f32[128,2048]{0,1:T(8,128)} %collective-permute-done.23), channel_id=1, source_target_pairs={{0,15},{1,0},{2,1},{3,2},{4,3},{5,4},{6,5},{7,6},{8,7},{9,8},{10,9... | collective-permute-start | bytes 3145736 | tf_op jit(solution)/shard_map/ppermute | solution.py:63
  822.2 28.4 %collective-permute-start.26 = (f32[128,2048]{0,1:T(8,128)}, f32[128,2048]{0,1:T(8,128)}, u32[]{:S(2)}, u32[]{:S(2)}) collective-permute-start(f32[128,2048]{0,1:T(8,128)} %collective-permute-done.24), channel_id=1, source_target_pairs={{0,1},{1,2},{2,3},{3,4},{4,5},{5,6},{6,7},{7,8},{8,9},{9,10},{10,1... | collective-permute-start | bytes 3145736 | tf_op jit(solution)/shard_map/ppermute | solution.py:60
  840.2 23.3 %collective-permute-start.27 = (f32[128,2048]{0,1:T(8,128)}, f32[128,2048]{0,1:T(8,128)}, u32[]{:S(2)}, u32[]{:S(2)}) collective-permute-start(f32[128,2048]{0,1:T(8,128)} %collective-permute-done.25), channel_id=1, source_target_pairs={{0,15},{1,0},{2,1},{3,2},{4,3},{5,4},{6,5},{7,6},{8,7},{9,8},{10,9... | collective-permute-start | bytes 3145736 | tf_op jit(solution)/shard_map/ppermute | solution.py:63
  850.6 25.2 %collective-permute-start.28 = (f32[128,2048]{0,1:T(8,128)}, f32[128,2048]{0,1:T(8,128)}, u32[]{:S(2)}, u32[]{:S(2)}) collective-permute-start(f32[128,2048]{0,1:T(8,128)} %collective-permute-done.26), channel_id=1, source_target_pairs={{0,1},{1,2},{2,3},{3,4},{4,5},{5,6},{6,7},{7,8},{8,9},{9,10},{10,1... | collective-permute-start | bytes 3145736 | tf_op jit(solution)/shard_map/ppermute | solution.py:60
  863.5 22.5 %collective-permute-start.29 = (f32[128,2048]{0,1:T(8,128)}, f32[128,2048]{0,1:T(8,128)}, u32[]{:S(2)}, u32[]{:S(2)}) collective-permute-start(f32[128,2048]{0,1:T(8,128)} %collective-permute-done.27), channel_id=1, source_target_pairs={{0,15},{1,0},{2,1},{3,2},{4,3},{5,4},{6,5},{7,6},{8,7},{9,8},{10,9... | collective-permute-start | bytes 3145736 | tf_op jit(solution)/shard_map/ppermute | solution.py:63
  875.8 21.4 %collective-permute-start.30 = (f32[128,2048]{0,1:T(8,128)}, f32[128,2048]{0,1:T(8,128)}, u32[]{:S(2)}, u32[]{:S(2)}) collective-permute-start(f32[128,2048]{0,1:T(8,128)} %collective-permute-done.28), channel_id=1, source_target_pairs={{0,1},{1,2},{2,3},{3,4},{4,5},{5,6},{6,7},{7,8},{8,9},{9,10},{10,1... | collective-permute-start | bytes 3145736 | tf_op jit(solution)/shard_map/ppermute | solution.py:60
  892.0 126.1 %copy-start.25 = (f32[128,128]{1,0:T(8,128)S(1)}, f32[128,128]{1,0:T(8,128)}, u32[]{:S(2)}) copy-start(f32[128,128]{1,0:T(8,128)} %get-tuple-element.136) | copy-start | bytes 196612
  899.9 199.3 %copy-start.24 = (f32[128,128]{1,0:T(8,128)S(1)}, f32[128,128]{1,0:T(8,128)}, u32[]{:S(2)}) copy-start(f32[128,128]{1,0:T(8,128)} %get-tuple-element.134) | copy-start | bytes 196612
  899.9 199.5 %copy-start.26 = (f32[128,128]{1,0:T(8,128)S(1)}, f32[128,128]{1,0:T(8,128)}, u32[]{:S(2)}) copy-start(f32[128,128]{1,0:T(8,128)} %get-tuple-element.132) | copy-start | bytes 196612
  912.4 190.2 %copy-start.27 = (f32[128,128]{1,0:T(8,128)S(1)}, f32[128,128]{1,0:T(8,128)}, u32[]{:S(2)}) copy-start(f32[128,128]{1,0:T(8,128)} %get-tuple-element.130) | copy-start | bytes 196612
  912.4 191.8 %copy-start.28 = (f32[128,128]{1,0:T(8,128)S(1)}, f32[128,128]{1,0:T(8,128)}, u32[]{:S(2)}) copy-start(f32[128,128]{1,0:T(8,128)} %get-tuple-element.128) | copy-start | bytes 196612
  912.4 193.4 %copy-start.29 = (f32[128,128]{1,0:T(8,128)S(1)}, f32[128,128]{1,0:T(8,128)}, u32[]{:S(2)}) copy-start(f32[128,128]{1,0:T(8,128)} %get-tuple-element.126) | copy-start | bytes 196612
  912.4 16.5 %collective-permute-start.32 = (f32[128,2048]{0,1:T(8,128)S(1)}, f32[128,2048]{0,1:T(8,128)S(1)}, u32[]{:S(2)}, u32[]{:S(2)}) collective-permute-start(f32[128,2048]{0,1:T(8,128)S(1)} %bitcast_add_fusion), channel_id=1, source_target_pairs={{0,32},{16,48},{32,0},{48,16},{64,96},{80,112},{96,64},{112,80},{1... | collective-permute-start | bytes 3145736 | tf_op jit(solution)/shard_map/ppermute | solution.py:14
  929.7 135.8 %all-gather.24.cloned.1.call-start = ((), (), s32[]{:S(2)}) async-start(), calls=%async_computation.7 | async-start | bytes 1114112 | tf_op jit(solution)/shard_map/all_gather | solution.py:22
  1017.8 127.6 %all-gather.26.cloned.1.call-start = ((), (), s32[]{:S(2)}) async-start(), calls=%async_computation.8 | async-start | bytes 1114112 | tf_op jit(solution)/shard_map/all_gather | solution.py:22
  (11 other events, 12.5 us)
Sparse Core Ops, SparseCore 0:
  11.0 50.7 all-gather.9
  92.0 47.5 all-gather.11
  170.7 47.5 all-gather.13
  462.9 49.2 all-gather.15
  543.4 47.5 all-gather.17
  623.3 47.5 all-gather.19
  929.8 49.4 all-gather.21
  1017.9 47.5 all-gather.23
  1097.8 47.5 all-gather.25
